TPU v7x, 32 devices: a whole 2x2x4 slice. The times are simulated.
32 devices in a mesh: prow: 4 (over x, core), pcol: 8 (over z, y).
Axes of the slice: x: 2, y: 2, z: 4, core: 2. Of those that a mesh axis runs over, the one named last changes fastest.
Arguments:
- features: bfloat16 [8192, 512], P(('prow', 'pcol')), may hold values from -6 to 6
- tile_values: bfloat16 [4, 8, 128, 128, 128], P('prow', 'pcol'), may hold values from 0.0009994507 to 1
- tile_rows: int32 [4, 8, 128], P('prow', 'pcol'), may hold values from 0 to 15, as said below
- tile_cols: int32 [4, 8, 128], P('prow', 'pcol'), may hold values from 0 to 7, as said below
- tile_count: int32 [4, 8], P('prow', 'pcol'), may hold values from 32 to 128, as said below
- hub_local: int32 [4, 8, 8], P('prow', 'pcol'), may hold values from 0 to 255, as said below
- hub_edges: bfloat16 [8192, 256], P(('prow', 'pcol')), may hold values from 0.5 to 2
- w_self: bfloat16 [512, 512], replicated, may hold values from -0.25 to 0.25
- w_neigh: bfloat16 [512, 512], replicated, may hold values from -12 to 12
- bias: float32 [512], replicated, may hold values from -3 to 3
- cotangent: bfloat16 [8192, 512], P(('prow', 'pcol')), may hold values from -6 to 6
Outputs:
- activations: bfloat16 [8192, 512], P(('prow', 'pcol'))
- grad_features: bfloat16 [8192, 512], P(('prow', 'pcol'))
- grad_w_self: float32 [512, 512], replicated
- grad_w_neigh: float32 [512, 512], replicated
- grad_bias: float32 [512], replicated
Inputs may be any that keep to these rules, and one draw needn't show every extreme that they name: On partition (i, j) the live slots (s < tile_count[i, j]) name distinct (tile_rows, tile_cols) pairs; slots 0 and 1 are always live. `tile_cols`: see tile_rows. `tile_count`: each partition's count is 128, 64 or 32. `hub_local`: distinct on each device.
All inputs are finite; a program needn't handle non-finite values.
Results may differ from a plain program's by a relative error of at most 0.008.
Values may be sent and summed in bfloat16 or wider, within the bound.
No kernel may reach another device: no remote copies, remote signals or barrier semaphores. Data moves between devices by JAX's collectives and lax.ppermute only.
A program may use at most 128 MiB of HBM per device.

v0:
```python
import math

import jax
import jax.numpy as jnp
from jax import lax
from jax.sharding import PartitionSpec as P


def per_device(
    features,
    tile_values,
    tile_rows,
    tile_cols,
    tile_count,
    hub_local,
    hub_edges,
    w_self,
    w_neigh,
    bias,
    cotangent,
):
    vertex_count, feat_width = features.shape
    tile_edge = tile_values.shape[-1]
    slot_count = tile_values.shape[2]
    prow_size = lax.axis_size("prow")
    pcol_size = lax.axis_size("pcol")
    row_tiles = pcol_size * vertex_count // tile_edge
    col_tiles = prow_size * vertex_count // tile_edge
    block_count = vertex_count // tile_edge
    active_flat = jnp.arange(slot_count, dtype=jnp.int32) < tile_count.reshape(())
    tile_blocks = tile_values.reshape(block_count, slot_count // block_count, tile_edge, tile_edge)
    row_ids = tile_rows.reshape(block_count, slot_count // block_count)
    col_ids = tile_cols.reshape(block_count, slot_count // block_count)
    active = active_flat.reshape(block_count, slot_count // block_count)
    source_cols = lax.all_gather(features, "prow", axis=0, tiled=True).reshape(
        col_tiles, tile_edge, feat_width
    )

    def forward_block(carry, block):
        row_acc, deg_acc = carry
        tiles_here, row_here, col_here, keep_here = block
        picked = jnp.take(source_cols, col_here, axis=0)
        product = jnp.einsum("stk,skf->stf", tiles_here, picked, preferred_element_type=jnp.float32)
        row_acc = row_acc.at[row_here].add(
            jnp.where(keep_here[:, None, None], product, jnp.float32(0.0))
        )
        row_weight = jnp.sum(tiles_here, axis=2, dtype=jnp.float32)
        deg_acc = deg_acc.at[row_here].add(
            jnp.where(keep_here[:, None], row_weight, jnp.float32(0.0))
        )
        return ((row_acc, deg_acc), None)

    start = (
        jnp.zeros((row_tiles, tile_edge, feat_width), jnp.float32),
        jnp.zeros((row_tiles, tile_edge), jnp.float32),
    )
    (row_acc, deg_acc), _ = lax.scan(forward_block, start, (tile_blocks, row_ids, col_ids, active))
    own_sums, own_deg = (
        lax.psum_scatter(
            row_acc.reshape(row_tiles * tile_edge, feat_width),
            "pcol",
            scatter_dimension=0,
            tiled=True,
        ),
        lax.psum_scatter(
            deg_acc.reshape(row_tiles * tile_edge), "pcol", scatter_dimension=0, tiled=True
        ),
    )
    hub_ids = hub_local.reshape(-1)
    hub_rows = jnp.take(features, hub_ids, axis=0)
    hub_features = lax.all_gather(hub_rows, ("prow", "pcol"), axis=0, tiled=True)
    hub_sum = jnp.dot(hub_edges, hub_features, preferred_element_type=jnp.float32)
    degree = own_deg + jnp.sum(hub_edges, axis=1, dtype=jnp.float32)
    aggregate = ((own_sums + hub_sum) / degree[:, None]).astype(jnp.bfloat16)
    pre = (
        jnp.dot(features, w_self, preferred_element_type=jnp.float32)
        + jnp.dot(aggregate, w_neigh, preferred_element_type=jnp.float32)
        + bias[None, :]
    )
    sigma = jax.nn.sigmoid(pre)
    activations = (pre * sigma).astype(jnp.bfloat16)
    dpre = cotangent.astype(jnp.float32) * sigma * (1.0 + pre * (1.0 - sigma))
    dpre_b = dpre.astype(jnp.bfloat16)
    total_rows = prow_size * pcol_size * vertex_count
    factor = 1.0 / math.sqrt(total_rows)
    self_part = jnp.dot(features.T, dpre_b, preferred_element_type=jnp.float32)
    neigh_part = jnp.dot(aggregate.T, dpre_b, preferred_element_type=jnp.float32)
    bias_part = jnp.sum(dpre, axis=0)
    self_total, neigh_total, bias_total = lax.psum(
        (self_part, neigh_part, bias_part), ("prow", "pcol")
    )
    grad_w_self = self_total * factor
    grad_w_neigh = neigh_total * factor
    grad_bias = bias_total * factor
    dagg = jnp.dot(dpre_b, w_neigh.T, preferred_element_type=jnp.float32)
    scaled = (dagg / degree[:, None]).astype(jnp.bfloat16)
    target_rows = lax.all_gather(scaled, "pcol", axis=0, tiled=True).reshape(
        row_tiles, tile_edge, feat_width
    )

    def backward_block(back_acc, block):
        tiles_here, row_here, col_here, keep_here = block
        picked = jnp.take(target_rows, row_here, axis=0)
        product = jnp.einsum("stk,stf->skf", tiles_here, picked, preferred_element_type=jnp.float32)
        back_acc = back_acc.at[col_here].add(
            jnp.where(keep_here[:, None, None], product, jnp.float32(0.0))
        )
        return (back_acc, None)

    back_acc, _ = lax.scan(
        backward_block,
        jnp.zeros((col_tiles, tile_edge, feat_width), jnp.float32),
        (tile_blocks, row_ids, col_ids, active),
    )
    back_rows = lax.psum_scatter(
        back_acc.reshape(col_tiles * tile_edge, feat_width).astype(jnp.bfloat16),
        "prow",
        scatter_dimension=0,
        tiled=True,
    ).astype(jnp.float32)
    hub_part = jnp.dot(hub_edges.T, scaled, preferred_element_type=jnp.float32)
    own_hubs = lax.psum_scatter(hub_part, ("prow", "pcol"), scatter_dimension=0, tiled=True)
    one_hot = (jnp.arange(vertex_count, dtype=jnp.int32)[:, None] == hub_ids[None, :]).astype(
        jnp.float32
    )
    hub_back = jnp.dot(one_hot, own_hubs, precision=lax.Precision.HIGHEST)
    grad_features = (
        jnp.dot(dpre_b, w_self.T, preferred_element_type=jnp.float32) + back_rows + hub_back
    ).astype(jnp.bfloat16)
    return (activations, grad_features, grad_w_self, grad_w_neigh, grad_bias)


def solution(mesh):
    in_specs = (
        P(("prow", "pcol"), None),
        P("prow", "pcol", None, None, None),
        P("prow", "pcol", None),
        P("prow", "pcol", None),
        P("prow", "pcol"),
        P("prow", "pcol", None),
        P(("prow", "pcol"), None),
        P(),
        P(),
        P(),
        P(("prow", "pcol"), None),
    )
    out_specs = (P(("prow", "pcol"), None), P(("prow", "pcol"), None), P(), P(), P())
    return jax.shard_map(
        per_device, mesh=mesh, in_specs=in_specs, out_specs=out_specs, check_vma=False
    )
```

profile of v0, /device:TPU:0, one launch (start us, length us, event | category | flops | bytes accessed | tf_op | source)
XLA Modules:
  0.0 608.5 jit_solution(5950233204561062805)
XLA Ops:
  11.9 17.1 %all-gather.3.cloned.1.call-done = bf16[1024,512]{1,0:T(8,128)(2,1)} async-done(((bf16[256,512]{1,0:T(8,128)(2,1)}), bf16[1024,512]{1,0:T(8,128)(2,1)}) %all-gather.3.cloned.1.call-update) | async-done | bytes 1048592 | tf_op jit(solution)/shard_map/all_gather | solution.py:35
  31.5 114.6 %while.22 = (s32[]{:T(128)}, f32[16,128,512]{2,1,0:T(8,128)}, f32[16,128]{1,0:T(8,128)S(1)}, s32[2,64]{1,0:T(2,128)S(1)}, pred[2,64]{1,0:T(4,128)(4,1)S(1)}, /*i...) while((s32[]{:T(128)}, f32[16,128,512]{2,1,0:T(8,128)}, ...), condition=%wide.region_4.5_spmd, body=%wide.region_0.4_spmd.sunk | while | flops 1088431872 | bytes 96549816 | solution.py:57
  31.5 5.5 gather_fusion
  37.1 12.1 %convolution_select_fusion.4 = f32[64,128,512]{2,1,0:T(8,128)} fusion(bf16[64,128,512]{2,1,0:T(8,128)(2,1)} %gather_fusion, pred[64]{0:T(512)(128)(4,1)S(1)} %compare_and_fusion.5, pred[64]{0:T(512)(128)(4,1)S(1)} %dynamic-slice_bitcast_fusion.4, bf16[2,64,128,128]{3,2,1,0:T(8,128)(2,1)} %get-tuple-element.297, s32[]{:T(128)S(6)} %copy.45), kind=kOutput, calls=%fused_computation.6.clone.1 | convolution fusion | flops 1082130432 | bytes 27263108 | tf_op jit(solution)/shard_map/while/body/eval_jaxpr/stk,skf->stf/dot_general | solution.py:43
  49.2 36.7 %scatter_fusion = f32[16,128,512]{2,1,0:T(8,128)} fusion(f32[16,128,512]{2,1,0:T(8,128)} %get-tuple-element.283, s32[64]{0:T(128)S(1)} %get-tuple-element.261, f32[64,128,512]{2,1,0:T(8,128)} %convolution_select_fusion.4), kind=kCustom, calls=%fused_computation.3.clone.1 | custom fusion | flops 4194304 | bytes 50331904 | tf_op jit(solution)/shard_map/while/body/eval_jaxpr/scatter-add | solution.py:44
  89.1 5.5 gather_fusion
  94.6 12.1 %convolution_select_fusion.4 = f32[64,128,512]{2,1,0:T(8,128)} fusion(bf16[64,128,512]{2,1,0:T(8,128)(2,1)} %gather_fusion, pred[64]{0:T(512)(128)(4,1)S(1)} %compare_and_fusion.5, pred[64]{0:T(512)(128)(4,1)S(1)} %dynamic-slice_bitcast_fusion.4, bf16[2,64,128,128]{3,2,1,0:T(8,128)(2,1)} %get-tuple-element.297, s32[]{:T(128)S(6)} %copy.45), kind=kOutput, calls=%fused_computation.6.clone.1 | convolution fusion | flops 1082130432 | bytes 27263108 | tf_op jit(solution)/shard_map/while/body/eval_jaxpr/stk,skf->stf/dot_general | solution.py:43
  106.8 36.2 %scatter_fusion = f32[16,128,512]{2,1,0:T(8,128)} fusion(f32[16,128,512]{2,1,0:T(8,128)} %get-tuple-element.283, s32[64]{0:T(128)S(1)} %get-tuple-element.261, f32[64,128,512]{2,1,0:T(8,128)} %convolution_select_fusion.4), kind=kCustom, calls=%fused_computation.3.clone.1 | custom fusion | flops 4194304 | bytes 50331904 | tf_op jit(solution)/shard_map/while/body/eval_jaxpr/scatter-add | solution.py:44
  146.2 5.4 copy.35
  154.6 70.9 %all_gather.10 = bf16[256,512]{1,0:T(8,128)(2,1)S(1)} all-gather(bf16[8,512]{1,0:T(8,128)(2,1)S(1)} %broadcast_select_fusion), channel_id=1, replica_groups=mesh['prow'=4,'pcol'=8] {'prow','pcol'}, dimensions={0}, use_global_device_ids=true | all-gather | bytes 270336 | tf_op jit(solution)/shard_map/all_gather | solution.py:71
  225.8 18.6 %all-reduce = f32[2048]{0:T(1024)S(1)} all-reduce(f32[2048]{0:T(1024)S(1)} %bitcast.114), channel_id=3, replica_groups=mesh['prow'=4,'pcol'=8] {'pcol'}, use_global_device_ids=true, to_apply=%region_6.7.clone | all-reduce | flops 2048 | bytes 16384
  248.3 6.4 %copy.24 = bf16[1,1,128,128,128]{3,4,2,1,0:T(8,128)(2,1)} copy(bf16[1,1,128,128,128]{4,3,2,1,0:T(8,128)(2,1)} %bitcast.111) | data formatting | bytes 8388608 | tf_op args[1]
  257.5 39.7 %all-gather.5.cloned.1.call-done = bf16[2048,512]{0,1:T(8,128)(2,1)} async-done(((bf16[256,512]{0,1:T(8,128)(2,1)}), bf16[2048,512]{0,1:T(8,128)(2,1)}) %all-gather.5.cloned.1.call-update) | async-done | bytes 2097168 | tf_op jit(solution)/shard_map/all_gather | solution.py:97
  301.3 85.1 %while.23 = (s32[]{:T(128)}, f32[8,128,512]{2,1,0:T(8,128)S(1)}, s32[2,64]{1,0:T(2,128)S(1)}, pred[2,64]{1,0:T(4,128)(4,1)S(1)}, bf16[2,64,128,128]{2,3,1,0:T(8,...) while((s32[]{:T(128)}, f32[8,128,512]{2,1,0:T(8,128)S(1)}, ...), condition=%wide.region_10.11_spmd, body=%wide.region_8.10_spmd.sunk | while | flops 1086326528 | bytes 94378408 | solution.py:110
  301.4 7.3 %gather_fusion.1 = bf16[64,128,512]{2,1,0:T(8,128)(2,1)} fusion(bf16[16,128,512]{2,1,0:T(8,128)(2,1)} %get-tuple-element.324, s32[1024]{0:T(1024)S(1)} %pad_clamp_fusion.6), kind=kCustom, calls=%fused_computation.1.clone.1 | custom fusion | bytes 16777472 | tf_op jit(solution)/shard_map/while/body/eval_jaxpr/jit(_take)/gather | solution.py:103
  308.7 12.2 %convolution_select_fusion.5 = f32[64,128,512]{2,1,0:T(8,128)} fusion(bf16[64,128,512]{2,1,0:T(8,128)(2,1)} %gather_fusion.1, pred[64]{0:T(512)(128)(4,1)S(1)} %compare_and_fusion.6, pred[64]{0:T(512)(128)(4,1)S(1)} %dynamic-slice_bitcast_fusion.5, bf16[2,64,128,128]{2,3,1,0:T(8,128)(2,1)} %get-tuple-element.322, s32[]{:T(128)S(6)} %copy.53), kind=kOutput, calls=%fused_computation.30.clone.1 | convolution fusion | flops 1082130432 | bytes 27263108 | tf_op jit(solution)/shard_map/while/body/eval_jaxpr/stk,stf->skf/dot_general | solution.py:104
  320.9 23.0 %scatter_fusion.1 = f32[8,128,512]{2,1,0:T(8,128)S(1)} fusion(f32[8,128,512]{2,1,0:T(8,128)S(1)} %get-tuple-element.311, s32[64]{0:T(128)S(1)} %get-tuple-element.270, f32[64,128,512]{2,1,0:T(8,128)} %convolution_select_fusion.5), kind=kCustom, calls=%fused_computation.5.clone.1 | custom fusion | flops 4194304 | bytes 50331904 | tf_op jit(solution)/shard_map/while/body/eval_jaxpr/scatter-add | solution.py:105
  344.0 7.1 %gather_fusion.1 = bf16[64,128,512]{2,1,0:T(8,128)(2,1)} fusion(bf16[16,128,512]{2,1,0:T(8,128)(2,1)} %get-tuple-element.324, s32[1024]{0:T(1024)S(1)} %pad_clamp_fusion.6), kind=kCustom, calls=%fused_computation.1.clone.1 | custom fusion | bytes 16777472 | tf_op jit(solution)/shard_map/while/body/eval_jaxpr/jit(_take)/gather | solution.py:103
  351.2 12.2 %convolution_select_fusion.5 = f32[64,128,512]{2,1,0:T(8,128)} fusion(bf16[64,128,512]{2,1,0:T(8,128)(2,1)} %gather_fusion.1, pred[64]{0:T(512)(128)(4,1)S(1)} %compare_and_fusion.6, pred[64]{0:T(512)(128)(4,1)S(1)} %dynamic-slice_bitcast_fusion.5, bf16[2,64,128,128]{2,3,1,0:T(8,128)(2,1)} %get-tuple-element.322, s32[]{:T(128)S(6)} %copy.53), kind=kOutput, calls=%fused_computation.30.clone.1 | convolution fusion | flops 1082130432 | bytes 27263108 | tf_op jit(solution)/shard_map/while/body/eval_jaxpr/stk,stf->skf/dot_general | solution.py:104
  363.4 23.0 %scatter_fusion.1 = f32[8,128,512]{2,1,0:T(8,128)S(1)} fusion(f32[8,128,512]{2,1,0:T(8,128)S(1)} %get-tuple-element.311, s32[64]{0:T(128)S(1)} %get-tuple-element.270, f32[64,128,512]{2,1,0:T(8,128)} %convolution_select_fusion.5), kind=kCustom, calls=%fused_computation.5.clone.1 | custom fusion | flops 4194304 | bytes 50331904 | tf_op jit(solution)/shard_map/while/body/eval_jaxpr/scatter-add | solution.py:105
  389.9 38.7 %psum.23 = f32[512]{0:T(512)S(1)} all-reduce(f32[512]{0:T(512)S(1)} %get-tuple-element.160), channel_id=1, replica_groups=mesh['prow'=4,'pcol'=8] {'prow','pcol'}, use_global_device_ids=true, to_apply=%region_16.17 | all-reduce | flops 512 | bytes 4096 | tf_op jit(solution)/shard_map/psum | solution.py:89
  429.2 6.8 %all-reduce.4.cloned.1.call-done = (f32[512,512]{0,1:T(8,128)}, f32[512,512]{0,1:T(8,128)}) async-done(((f32[512,512]{0,1:T(8,128)}, f32[512,512]{0,1:T(8,128)}), (f32[512,512]{0,1:T(8,128)}, f32[512,512]{0,1:T(8,128)})) %all-reduce.4.cloned.1.call-update) | async-done | bytes 2097168 | tf_op jit(solution)/shard_map/psum | solution.py:89
  440.4 21.6 %reduce-scatter.8.cloned.1.call-done = bf16[256,512]{1,0:T(8,128)(2,1)} async-done(((bf16[1024,512]{1,0:T(8,128)(2,1)}), bf16[256,512]{1,0:T(8,128)(2,1)}) %reduce-scatter.8.cloned.1.call-update) | async-done | bytes 262160 | tf_op jit(solution)/shard_map/reduce_scatter | solution.py:115
  463.3 136.6 %reduce-scatter.10.cloned.1.call-done = f32[8,512]{1,0:T(8,128)} async-done(((f32[256,512]{1,0:T(8,128)}), f32[8,512]{1,0:T(8,128)}) %reduce-scatter.10.cloned.1.call-update) | async-done | bytes 16400
  (90 shorter events, 37.9 us)
Async XLA Ops:
  7.2 238.7 %copy-start = (bf16[512,512]{1,0:T(8,128)(2,1)S(1)}, bf16[512,512]{1,0:T(8,128)(2,1)}, u32[]{:S(2)}) copy-start(bf16[512,512]{1,0:T(8,128)(2,1)} %param.23) | copy-start | bytes 1572868
  7.2 21.8 %all-gather.3.cloned.1.call-start = ((), (), s32[]{:S(2)}) async-start(), calls=%async_computation.3 | async-start | bytes 1310720 | tf_op jit(solution)/shard_map/all_gather | solution.py:35
  7.9 236.6 %reduce-scatter.6.cloned.1.call-start = ((), (), s32[]{:S(2)}) async-start(), calls=%async_computation.4 | async-start | bytes 4718592 | tf_op jit(solution)/shard_map/reduce_scatter | solution.py:59
  29.0 2.5 copy-start.2
  146.2 5.4 copy-start.9
  151.6 0.7 copy-start.6
  151.6 1.0 copy-start.3
  151.6 1.5 copy-start.11
  151.6 2.8 copy-start.5
  151.6 73.9 %copy-start.4 = (bf16[512,512]{1,0:T(8,128)(2,1)S(1)}, bf16[512,512]{1,0:T(8,128)(2,1)}, u32[]{:S(2)}) copy-start(bf16[512,512]{1,0:T(8,128)(2,1)} %param.22) | copy-start | bytes 1572868
  151.6 94.3 %copy-start.7 = (bf16[256,512]{1,0:T(8,128)(2,1)S(1)}, bf16[256,512]{1,0:T(8,128)(2,1)}, u32[]{:S(2)}) copy-start(bf16[256,512]{1,0:T(8,128)(2,1)} %param.25) | copy-start | bytes 786436
  151.6 94.3 %copy-start.8 = (f32[512]{0:T(512)S(1)}, f32[512]{0:T(512)}, u32[]{:S(2)}) copy-start(f32[512]{0:T(512)} %param.24) | copy-start | bytes 6148
  151.7 145.5 %all-gather.5.cloned.1.call-start = ((), (), s32[]{:S(2)}) async-start(), calls=%async_computation.5 | async-start | bytes 2359296 | tf_op jit(solution)/shard_map/all_gather | solution.py:97
  248.2 187.7 %all-reduce.4.cloned.1.call-start = ((), (), s32[]{:S(2)}) async-start(), calls=%async_computation.8 | async-start | bytes 4194304 | tf_op jit(solution)/shard_map/psum | solution.py:89
  257.2 44.1 %copy-start.10 = (pred[2,64]{1,0:T(4,128)(4,1)S(1)}, pred[2,64]{1,0:T(4,128)(4,1)}, u32[]{:S(2)}) copy-start(pred[2,64]{1,0:T(4,128)(4,1)} %copy-done.9) | copy-start | bytes 388
  257.2 204.7 %reduce-scatter.8.cloned.1.call-start = ((), (), s32[]{:S(2)}) async-start(), calls=%async_computation.6 | async-start | bytes 1310720 | tf_op jit(solution)/shard_map/reduce_scatter | solution.py:115
  387.6 212.3 %reduce-scatter.10.cloned.1.call-start = ((), (), s32[]{:S(2)}) async-start(), calls=%async_computation.7 | async-start | bytes 540672
  435.9 165.7 %copy-start.1 = (bf16[512,512]{1,0:T(8,128)(2,1)S(1)}, bf16[512,512]{1,0:T(8,128)(2,1)}, u32[]{:S(2)}) copy-start(bf16[512,512]{1,0:T(8,128)(2,1)} %param.23) | copy-start | bytes 1572868
Sparse Core Ops, SparseCore 0:
  9.5 19.4 all-gather.2
  151.8 91.2 reduce-scatter.5
  248.3 48.7 all-gather.4
  303.1 132.7 all-reduce.3
  438.3 23.6 reduce-scatter.7
  464.1 135.7 reduce-scatter.9
where the time goes:
time: 610 us; the launch traced here: 608 us
  waiting for transfers between devices  222 us (36%)
  other arithmetic  132 us (22%)
  blocking collectives  128 us (21%)
  matrix products  59.4 us (10%)
  local copies, waits for them, and re-layouts  50.2 us (8%)
  between operations  15.6 us (3%)
    unnamed x7, waiting for transfers between devices  137 us
    scatter-add x2, other arithmetic, forward_block(): row_acc.at[row_here]  72.9 us
    all_gather x1, blocking collectives, per_device(): lax.all_gather(hub_rows, ('prow', 'pcol'), axis=0, tiled=True)  70.9 us
    scatter-add x2, other arithmetic, backward_block(): back_acc.at[col_here]  46.1 us
    all_gather x1, waiting for transfers between devices, per_device(): lax.all_gather(scaled, 'pcol', axis=0, tiled=True)  39.7 us
    psum x1, blocking collectives, per_device(): lax.psum((self_part, neigh_part, bias_part), ('prow', 'pcol'))  38.7 us
    dot_general x2, matrix products, backward_block(): jnp.einsum('stk,stf->skf', tiles_here, picked, preferred_element_type=jnp...  24.4 us
    dot_general x2, matrix products, forward_block(): jnp.einsum('stk,skf->stf', tiles_here, picked, preferred_element_type=jnp...  24.3 us
  transfers between devices with their start and end apart: 6, of which 5 were waited for; matrix products, arithmetic and copies ran while one was open for 19% of the time, Pallas kernels for 0%

commit v1 on v0

v1 whole, which is shorter than its diff:
```python
import math

import jax
import jax.numpy as jnp
from jax import lax
from jax.sharding import PartitionSpec as P


def per_device(
    features,
    tile_values,
    tile_rows,
    tile_cols,
    tile_count,
    hub_local,
    hub_edges,
    w_self,
    w_neigh,
    bias,
    cotangent,
):
    vertex_count, feat_width = features.shape
    tile_edge = tile_values.shape[-1]
    slot_count = tile_values.shape[2]
    hub_count = hub_local.shape[-1]
    prow_size = lax.axis_size("prow")
    pcol_size = lax.axis_size("pcol")
    row_tiles = pcol_size * vertex_count // tile_edge
    col_tiles = prow_size * vertex_count // tile_edge
    positions = row_tiles * col_tiles

    tiles = tile_values.reshape(slot_count, tile_edge, tile_edge)
    live = jnp.arange(slot_count, dtype=jnp.int32) < tile_count.reshape(())
    pos = tile_rows.reshape(slot_count) * col_tiles + tile_cols.reshape(slot_count)
    place = (pos[:, None] == jnp.arange(positions, dtype=jnp.int32)[None, :]) & live[:, None]
    dense = jnp.einsum(
        "sp,sab->pab", place.astype(jnp.bfloat16), tiles, preferred_element_type=jnp.bfloat16
    )
    adj = (
        dense.reshape(row_tiles, col_tiles, tile_edge, tile_edge)
        .transpose(0, 2, 1, 3)
        .reshape(row_tiles * tile_edge, col_tiles * tile_edge)
    )

    hub_ids = hub_local.reshape(hub_count)
    hub_rows = jnp.take(features, hub_ids, axis=0)
    payload = jnp.concatenate([features, hub_rows], axis=0)
    gathered = lax.all_gather(payload, "prow", axis=0, tiled=False)
    source_cols = gathered[:, :vertex_count].reshape(prow_size * vertex_count, feat_width)
    hub_col = gathered[:, vertex_count:]
    hub_all = lax.all_gather(
        hub_col.reshape(prow_size * hub_count, feat_width), "pcol", axis=0, tiled=True
    )
    hub_features = (
        hub_all.reshape(pcol_size, prow_size, hub_count, feat_width)
        .transpose(1, 0, 2, 3)
        .reshape(prow_size * pcol_size * hub_count, feat_width)
    )

    row_sums = jnp.dot(adj, source_cols, preferred_element_type=jnp.float32)
    row_deg = jnp.sum(adj, axis=1, dtype=jnp.float32)
    deg_row = jnp.pad(
        row_deg.reshape(pcol_size, 1, vertex_count), ((0, 0), (0, 0), (0, feat_width - vertex_count))
    )
    packed = jnp.concatenate(
        [row_sums.reshape(pcol_size, vertex_count, feat_width), deg_row], axis=1
    )
    reduced = lax.psum_scatter(packed, "pcol", scatter_dimension=0, tiled=True)
    own_sums = reduced[0, :vertex_count]
    own_deg = reduced[0, vertex_count, :vertex_count]

    hub_sum = jnp.dot(hub_edges, hub_features, preferred_element_type=jnp.float32)
    degree = own_deg + jnp.sum(hub_edges, axis=1, dtype=jnp.float32)
    aggregate = ((own_sums + hub_sum) / degree[:, None]).astype(jnp.bfloat16)
    pre = (
        jnp.dot(features, w_self, preferred_element_type=jnp.float32)
        + jnp.dot(aggregate, w_neigh, preferred_element_type=jnp.float32)
        + bias[None, :]
    )
    sigma = jax.nn.sigmoid(pre)
    activations = (pre * sigma).astype(jnp.bfloat16)
    dpre = cotangent.astype(jnp.float32) * sigma * (1.0 + pre * (1.0 - sigma))
    dpre_b = dpre.astype(jnp.bfloat16)
    total_rows = prow_size * pcol_size * vertex_count
    factor = 1.0 / math.sqrt(total_rows)
    self_part = jnp.dot(features.T, dpre_b, preferred_element_type=jnp.float32)
    neigh_part = jnp.dot(aggregate.T, dpre_b, preferred_element_type=jnp.float32)
    bias_part = jnp.sum(dpre, axis=0)
    grad_pack = jnp.concatenate(
        [
            self_part,
            neigh_part,
            jnp.broadcast_to(bias_part[None, :], (8, feat_width)),
        ],
        axis=0,
    )
    grad_total = lax.psum(grad_pack, ("prow", "pcol"))
    grad_w_self = grad_total[:feat_width] * factor
    grad_w_neigh = grad_total[feat_width : 2 * feat_width] * factor
    grad_bias = grad_total[2 * feat_width] * factor

    dagg = jnp.dot(dpre_b, w_neigh.T, preferred_element_type=jnp.float32)
    scaled = (dagg / degree[:, None]).astype(jnp.bfloat16)
    target_rows = lax.all_gather(scaled, "pcol", axis=0, tiled=True)
    back = lax.dot_general(
        adj, target_rows, (((0,), (0,)), ((), ())), preferred_element_type=jnp.float32
    )

    hub_part = jnp.dot(hub_edges.T, scaled, preferred_element_type=jnp.float32)
    hub_by_col = hub_part.reshape(prow_size, pcol_size, hub_count, feat_width).transpose(1, 0, 2, 3)
    hub_col_sum = lax.psum_scatter(hub_by_col, "pcol", scatter_dimension=0, tiled=True)
    back_ext = jnp.concatenate(
        [
            back.reshape(prow_size, vertex_count, feat_width),
            hub_col_sum.reshape(prow_size, hub_count, feat_width),
        ],
        axis=1,
    ).astype(jnp.bfloat16)
    back_own = lax.psum_scatter(back_ext, "prow", scatter_dimension=0, tiled=True)
    back_rows = back_own[0, :vertex_count].astype(jnp.float32)
    own_hubs = back_own[0, vertex_count:]
    one_hot = (jnp.arange(vertex_count, dtype=jnp.int32)[:, None] == hub_ids[None, :]).astype(
        jnp.bfloat16
    )
    hub_back = jnp.dot(one_hot, own_hubs, preferred_element_type=jnp.float32)
    grad_features = (
        jnp.dot(dpre_b, w_self.T, preferred_element_type=jnp.float32) + back_rows + hub_back
    ).astype(jnp.bfloat16)
    return (activations, grad_features, grad_w_self, grad_w_neigh, grad_bias)


def solution(mesh):
    in_specs = (
        P(("prow", "pcol"), None),
        P("prow", "pcol", None, None, None),
        P("prow", "pcol", None),
        P("prow", "pcol", None),
        P("prow", "pcol"),
        P("prow", "pcol", None),
        P(("prow", "pcol"), None),
        P(),
        P(),
        P(),
        P(("prow", "pcol"), None),
    )
    out_specs = (P(("prow", "pcol"), None), P(("prow", "pcol"), None), P(), P(), P())
    return jax.shard_map(
        per_device, mesh=mesh, in_specs=in_specs, out_specs=out_specs, check_vma=False
    )
```

time: 610 us -> 427 us (0.70)
  other arithmetic: 132 us -> 14.5 us
  blocking collectives: 128 us -> 32.2 us
  waiting for transfers between devices: 222 us -> 313 us
  matrix products: 59.4 us -> 25.4 us
  local copies, waits for them, and re-layouts: 50.2 us -> 25.4 us
    unnamed x7 -> x6, waiting for transfers between devices: 137 us -> 0.59 us
    psum x1, waiting for transfers between devices: 6.75 us -> 132 us  [per_device(): grad_total = lax.psum(grad_pack, ('prow', 'pcol'))]
    scatter-add x6 -> x0, other arithmetic: 121 us -> none  [the longest x2 72.9 us: forward_block(): row_acc.at[row_here]]
    reduce_scatter x2 -> x3, waiting for transfers between devices: 21.6 us -> 129 us  [the longest x1 58.3 us: per_device(): reduced = lax.psum_scatter(packed, 'pcol', scatter_dimension=0, tiled=True)]
    psum x1 -> x0, blocking collectives: 38.7 us -> none  [per_device(): lax.psum((self_part, neigh_part, bias_part), ('prow', 'pcol'))]
    all_gather x1, blocking collectives: 70.9 us -> 32.2 us  [per_device(): lax.all_gather(hub_col.reshape(prow_size * hub_count, feat_width), 'pcol'...]
    dot_general x5 -> x4, matrix products: 50.5 us -> 20.1 us  [the longest x1 8.74 us: per_device(): jnp.einsum('sp,sab->pab', place.astype(jnp.bfloat16), tiles, preferred_el...]
    gather x4 -> x0, local copies, waits for them, and re-layouts: 25.4 us -> none  [the longest x2 14.4 us: backward_block(): picked = jnp.take(target_rows, row_here, axis=0)]
  transfers between devices with their start and end apart: 6 -> 6, of which waited for: 5 -> 6; matrix products, arithmetic and copies ran while one was open for 19% -> 10% of each run, Pallas kernels for 0% -> 0%
where the time goes in v1:
time: 427 us; the launch traced here: 426 us
  waiting for transfers between devices  313 us (73%)
  blocking collectives  32.2 us (8%)
  local copies, waits for them, and re-layouts  25.4 us (6%)
  matrix products  25.4 us (6%)
  between operations  15 us (4%)
  other arithmetic  14.5 us (3%)
    psum x1, waiting for transfers between devices, per_device(): grad_total = lax.psum(grad_pack, ('prow', 'pcol'))  132 us
    reduce_scatter x1, waiting for transfers between devices, per_device(): reduced = lax.psum_scatter(packed, 'pcol', scatter_dimension=0, tiled=True)  58.3 us
    all_gather x1, waiting for transfers between devices, per_device(): target_rows = lax.all_gather(scaled, 'pcol', axis=0, tiled=True)  49.8 us
    reduce_scatter x1, waiting for transfers between devices, per_device(): lax.psum_scatter(hub_by_col, 'pcol', scatter_dimension=0, tiled=True)  47.6 us
    all_gather x1, blocking collectives, per_device(): lax.all_gather(hub_col.reshape(prow_size * hub_count, feat_width), 'pcol'...  32.2 us
    reduce_scatter x1, waiting for transfers between devices, per_device(): lax.psum_scatter(back_ext, 'prow', scatter_dimension=0, tiled=True)  22.9 us
    dot_general x1, matrix products, per_device(): jnp.einsum('sp,sab->pab', place.astype(jnp.bfloat16), tiles, preferred_el...  8.74 us
  transfers between devices with their start and end apart: 6, of which 6 were waited for; matrix products, arithmetic and copies ran while one was open for 10% of the time, Pallas kernels for 0%

profile of v1, /device:TPU:0, one launch (start us, length us, event | category | flops | bytes accessed | tf_op | source)
XLA Modules:
  0.0 426.4 jit_solution(4406606279071641449)
XLA Ops:
  8.6 1.6 gather_fusion
  10.2 1.7 pad_maximum_fusion.2
  13.3 8.7 %convert_reduce_fusion = (f32[16,128]{1,0:T(8,128)S(1)}, bf16[16,8,128,128]{3,1,2,0:T(8,128)(2,1)}) fusion(bf16[128,128,128]{2,1,0:T(8,128)(2,1)} %bitcast.106, s32[16,8]{1,0:T(8,128)S(1)} %multiply_add_fusion, s32[128]{0:T(128)S(1)} %add_bitcast_fusion, pred[128]{0:T(512)(128)(4,1)S(1)} %iota_compare_fusion.3), kind=kOutput, calls=%fused_computation.1 | convolution fusion | flops 541095936 | bytes 8397952 | tf_op jit(solution)/shard_map/sp,sab->pab/dot_general | solution.py:36
  22.1 7.4 %dot_general.50 = bf16[8,256,1024]{2,1,0:T(8,128)(2,1)} reshape(bf16[16,128,8,128]{3,2,1,0:T(8,128)(2,1)} %bitcast.103) | data formatting | bytes 8388608 | tf_op jit(solution)/shard_map/dot_general | solution.py:60
  29.5 2.2 all-gather.6.cloned.1.call-done
  31.7 1.3 slice.38
  33.0 4.5 %fusion.24 = f32[8,256,512]{2,1,0:T(8,128)S(1)} fusion(bf16[8,256,1024]{2,1,0:T(8,128)(2,1)} %dot_general.50, bf16[1024,512,1]{1,0,2:T(8,128)(2,1)S(1)} %bitcast.112), kind=kOutput, calls=%fused_computation.58 | convolution fusion | flops 2147483648 | bytes 9437184 | tf_op jit(solution)/shard_map/dot_general | solution.py:60
  37.5 2.7 select_maximum_fusion
  42.5 32.2 %all_gather.14 = bf16[256,512]{1,0:T(8,128)(2,1)S(1)} all-gather(bf16[32,512]{1,0:T(8,128)(2,1)S(1)} %slice_bitcast_fusion.2), channel_id=1, replica_groups=mesh['prow'=4,'pcol'=8] {'pcol'}, dimensions={0}, use_global_device_ids=true | all-gather | bytes 294912 | tf_op jit(solution)/shard_map/all_gather | solution.py:51
  74.8 58.3 %reduce-scatter.4.cloned.1.call-done = f32[1,257,512]{2,1,0:T(8,128)} async-done(((f32[8,257,512]{2,1,0:T(8,128)}), f32[1,257,512]{2,1,0:T(8,128)}) %reduce-scatter.4.cloned.1.call-update) | async-done | bytes 526352 | tf_op jit(solution)/shard_map/reduce_scatter | solution.py:68
  133.7 1.3 fusion.12
  135.0 1.2 fusion.22
  139.1 1.5 pad_maximum_fusion
  140.8 5.3 %copy.39 = bf16[256,8,8,128]{3,1,2,0:T(8,128)(2,1)} copy(bf16[256,8,8,128]{3,2,1,0:T(8,128)(2,1)} %bitcast.104) | data formatting | bytes 8388608
  146.2 6.5 %copy.26 = bf16[1024,2048]{1,0:T(8,128)(2,1)} copy(bf16[1024,2048]{0,1:T(8,128)(2,1)} %bitcast.105) | data formatting | bytes 8388608 | tf_op jit(solution)/shard_map/dot_general | solution.py:105
  152.7 47.6 %reduce-scatter.6.cloned.1.call-done = f32[1,4,8,512]{3,2,1,0:T(8,128)} async-done(((f32[8,4,8,512]{3,2,1,0:T(8,128)}), f32[1,4,8,512]{3,2,1,0:T(8,128)}) %reduce-scatter.6.cloned.1.call-update) | async-done | bytes 65552 | tf_op jit(solution)/shard_map/reduce_scatter | solution.py:111
  201.2 49.8 %all-gather.4.cloned.1.call-done = bf16[2048,512]{1,0:T(8,128)(2,1)} async-done(((bf16[256,512]{1,0:T(8,128)(2,1)}), bf16[2048,512]{1,0:T(8,128)(2,1)}) %all-gather.4.cloned.1.call-update) | async-done | bytes 2097168 | tf_op jit(solution)/shard_map/all_gather | solution.py:104
  251.0 5.2 %fusion.5 = bf16[4,256,512]{2,1,0:T(8,128)(2,1)S(1)} fusion(bf16[4,256,2048]{2,1,0:T(8,128)(2,1)} %bitcast.107, bf16[2048,512]{1,0:T(8,128)(2,1)} %all-gather.4.cloned.1.call-done), kind=kOutput, calls=%fused_computation.11 | convolution fusion | flops 2148007936 | bytes 7340032 | tf_op jit(solution)/shard_map/dot_general | solution.py:105
  257.3 132.0 %all-reduce.3.cloned.1.call-done = f32[1032,512]{1,0:T(8,128)} async-done(((f32[1032,512]{1,0:T(8,128)}), f32[1032,512]{1,0:T(8,128)}) %all-reduce.3.cloned.1.call-update) | async-done | bytes 2113552 | tf_op jit(solution)/shard_map/psum | solution.py:97
  389.4 1.3 slice_multiply_fusion.2
  390.7 3.1 slice_multiply_fusion
  393.8 22.9 %reduce-scatter.8.cloned.1.call-done = bf16[1,264,512]{2,1,0:T(8,128)(2,1)} async-done(((bf16[4,264,512]{2,1,0:T(8,128)(2,1)}), bf16[1,264,512]{2,1,0:T(8,128)(2,1)}) %reduce-scatter.8.cloned.1.call-update) | async-done | bytes 270352 | tf_op jit(solution)/shard_map/reduce_scatter | solution.py:119
  416.7 1.3 convolution_add_fusion.1
  417.9 1.6 fusion.13
  (49 shorter events, 10.1 us)
Async XLA Ops:
  7.2 127.8 %copy-start = (bf16[512,512]{1,0:T(8,128)(2,1)S(1)}, bf16[512,512]{1,0:T(8,128)(2,1)}, u32[]{:S(2)}) copy-start(bf16[512,512]{1,0:T(8,128)(2,1)} %param.19) | copy-start | bytes 1572868
  7.2 24.5 %all-gather.6.cloned.1.call-start = ((), (), s32[]{:S(2)}) async-start(), calls=%async_computation.8 | async-start | bytes 1351680 | tf_op jit(solution)/shard_map/all_gather | solution.py:48
  11.9 121.1 %reduce-scatter.4.cloned.1.call-start = ((), (), s32[]{:S(2)}) async-start(), calls=%async_computation.3 | async-start | bytes 4866048 | tf_op jit(solution)/shard_map/reduce_scatter | solution.py:68
  40.2 0.9 copy-start.4
  40.2 1.0 copy-start.1
  40.2 1.2 copy-start.2
  40.2 94.8 %copy-start.6 = (bf16[256,512]{1,0:T(8,128)(2,1)S(1)}, bf16[256,512]{1,0:T(8,128)(2,1)}, u32[]{:S(2)}) copy-start(bf16[256,512]{1,0:T(8,128)(2,1)} %param.21) | copy-start | bytes 786436
  40.2 94.8 %copy-start.7 = (f32[512]{0:T(512)S(1)}, f32[512]{0:T(512)}, u32[]{:S(2)}) copy-start(f32[512]{0:T(512)} %param.20) | copy-start | bytes 6148
  40.3 160.0 %reduce-scatter.6.cloned.1.call-start = ((), (), s32[]{:S(2)}) async-start(), calls=%async_computation.5 | async-start | bytes 589824 | tf_op jit(solution)/shard_map/reduce_scatter | solution.py:111
  136.6 1.2 copy-start.3
  137.8 113.3 %all-gather.4.cloned.1.call-start = ((), (), s32[]{:S(2)}) async-start(), calls=%async_computation.4 | async-start | bytes 2359296 | tf_op jit(solution)/shard_map/all_gather | solution.py:104
  138.3 251.0 %all-reduce.3.cloned.1.call-start = ((), (), s32[]{:S(2)}) async-start(), calls=%async_computation.7 | async-start | bytes 4227072 | tf_op jit(solution)/shard_map/psum | solution.py:97
  140.6 276.0 %reduce-scatter.8.cloned.1.call-start = ((), (), s32[]{:S(2)}) async-start(), calls=%async_computation.6 | async-start | bytes 1351680 | tf_op jit(solution)/shard_map/reduce_scatter | solution.py:119
  256.2 161.7 %copy-start.5 = (s32[1,1,8]{2,1,0:T(1,128)S(1)}, s32[1,1,8]{2,1,0:T(1,128)}, u32[]{:S(2)}) copy-start(s32[1,1,8]{2,1,0:T(1,128)} %param.16) | copy-start | bytes 100
Sparse Core Ops, SparseCore 0:
  12.1 19.5 all-gather.5
  40.4 92.5 reduce-scatter.3
  137.9 62.4 reduce-scatter.5
  202.9 48.0 all-gather.3
  256.4 132.9 all-reduce.2
  391.8 24.8 reduce-scatter.7

commit v2 on v1

--- a/solution.py
+++ b/solution.py
@@ -4,6 +4,31 @@
 import jax.numpy as jnp
 from jax import lax
 from jax.sharding import PartitionSpec as P
+
+
+def _pairwise_allreduce(flat, axes):
+    steps = []
+    for axis in axes:
+        size = lax.axis_size(axis)
+        bit = 1
+        while bit < size:
+            steps.append((axis, size, bit))
+            bit *= 2
+    x = flat
+    for axis, size, bit in steps:
+        upper = (lax.axis_index(axis) // bit) % 2 == 1
+        half = x.shape[0] // 2
+        low, high = x[:half], x[half:]
+        keep = jnp.where(upper, high, low)
+        send = jnp.where(upper, low, high)
+        perm = [(k, k ^ bit) for k in range(size)]
+        x = keep + lax.ppermute(send, axis, perm)
+    for axis, size, bit in reversed(steps):
+        upper = (lax.axis_index(axis) // bit) % 2 == 1
+        perm = [(k, k ^ bit) for k in range(size)]
+        other = lax.ppermute(x, axis, perm)
+        x = jnp.where(upper, jnp.concatenate([other, x]), jnp.concatenate([x, other]))
+    return x
 
 
 def per_device(
@@ -57,6 +82,13 @@
         .reshape(prow_size * pcol_size * hub_count, feat_width)
     )
 
+    edges_by_col = hub_edges.reshape(vertex_count, prow_size, pcol_size, hub_count).transpose(
+        2, 0, 1, 3
+    )
+    hub_cols = lax.all_to_all(edges_by_col, "pcol", 0, 0, tiled=True).reshape(
+        pcol_size * vertex_count, prow_size * hub_count
+    )
+
     row_sums = jnp.dot(adj, source_cols, preferred_element_type=jnp.float32)
     row_deg = jnp.sum(adj, axis=1, dtype=jnp.float32)
     deg_row = jnp.pad(
@@ -94,7 +126,9 @@
         ],
         axis=0,
     )
-    grad_total = lax.psum(grad_pack, ("prow", "pcol"))
+    grad_total = _pairwise_allreduce(grad_pack.reshape(-1), ("prow", "pcol")).reshape(
+        grad_pack.shape
+    )
     grad_w_self = grad_total[:feat_width] * factor
     grad_w_neigh = grad_total[feat_width : 2 * feat_width] * factor
     grad_bias = grad_total[2 * feat_width] * factor
@@ -106,9 +140,9 @@
         adj, target_rows, (((0,), (0,)), ((), ())), preferred_element_type=jnp.float32
     )
 
-    hub_part = jnp.dot(hub_edges.T, scaled, preferred_element_type=jnp.float32)
-    hub_by_col = hub_part.reshape(prow_size, pcol_size, hub_count, feat_width).transpose(1, 0, 2, 3)
-    hub_col_sum = lax.psum_scatter(hub_by_col, "pcol", scatter_dimension=0, tiled=True)
+    hub_col_sum = lax.dot_general(
+        hub_cols, target_rows, (((0,), (0,)), ((), ())), preferred_element_type=jnp.float32
+    )
     back_ext = jnp.concatenate(
         [
             back.reshape(prow_size, vertex_count, feat_width),

time: 427 us -> 270 us (0.63)
  waiting for transfers between devices: 313 us -> 126 us
  starting transfers between devices: 0.42 us -> 19.8 us
  local copies, waits for them, and re-layouts: 25.4 us -> 31.5 us
    psum x1 -> x0, waiting for transfers between devices: 132 us -> none  [per_device(): grad_total = lax.psum(grad_pack, ('prow', 'pcol'))]
    reduce_scatter x1 -> x0, waiting for transfers between devices: 47.6 us -> none  [per_device(): lax.psum_scatter(hub_by_col, 'pcol', scatter_dimension=0, tiled=True)]
    ppermute x0 -> x10, waiting for transfers between devices: none -> 33.5 us  [the longest x5 28.4 us: _pairwise_allreduce(): x = keep + lax.ppermute(send, axis, perm)]
    all_gather x1, waiting for transfers between devices: 49.8 us -> 21.4 us  [per_device(): target_rows = lax.all_gather(scaled, 'pcol', axis=0, tiled=True)]
    ppermute x0 -> x10, starting transfers between devices: none -> 14.5 us  [the longest x5 7.55 us: _pairwise_allreduce(): other = lax.ppermute(x, axis, perm)]
    reduce_scatter x1, waiting for transfers between devices: 22.9 us -> 10.7 us  [per_device(): lax.psum_scatter(back_ext, 'prow', scatter_dimension=0, tiled=True)]
    select_n x0 -> x12, other arithmetic: none -> 6.32 us  [the longest x7 5.91 us: _pairwise_allreduce(): jnp.where(upper, jnp.concatenate([other, x]), jnp.concatenate([x, other]))]
    all_to_all x0 -> x1, starting transfers between devices: none -> 5.13 us  [per_device(): lax.all_to_all(edges_by_col, 'pcol', 0, 0, tiled=True)]
  transfers between devices with their start and end apart: 6 -> 15, of which waited for: 6 -> 11; matrix products, arithmetic and copies ran while one was open for 10% -> 19% of each run, Pallas kernels for 0% -> 0%
where the time goes in v2:
time: 270 us; the launch traced here: 269 us
  waiting for transfers between devices  126 us (47%)
  blocking collectives  32.6 us (12%)
  local copies, waits for them, and re-layouts  31.5 us (12%)
  matrix products  26.5 us (10%)
  starting transfers between devices  19.8 us (7%)
  other arithmetic  18.4 us (7%)
  between operations  14.8 us (5%)
    reduce_scatter x1, waiting for transfers between devices, per_device(): reduced = lax.psum_scatter(packed, 'pcol', scatter_dimension=0, tiled=True)  57.8 us
    all_gather x1, blocking collectives, per_device(): lax.all_gather(hub_col.reshape(prow_size * hub_count, feat_width), 'pcol'...  32.6 us
    ppermute x5, waiting for transfers between devices, _pairwise_allreduce(): x = keep + lax.ppermute(send, axis, perm)  28.4 us
    all_gather x1, waiting for transfers between devices, per_device(): target_rows = lax.all_gather(scaled, 'pcol', axis=0, tiled=True)  21.4 us
    reduce_scatter x1, waiting for transfers between devices, per_device(): lax.psum_scatter(back_ext, 'prow', scatter_dimension=0, tiled=True)  10.7 us
    dot_general x1, matrix products, per_device(): jnp.einsum('sp,sab->pab', place.astype(jnp.bfloat16), tiles, preferred_el...  8.74 us
    ppermute x5, starting transfers between devices, _pairwise_allreduce(): other = lax.ppermute(x, axis, perm)  7.55 us
    dot_general x1, local copies, waits for them, and re-layouts, per_device(): row_sums = jnp.dot(adj, source_cols, preferred_element_type=jnp.float32)  7.32 us
  transfers between devices with their start and end apart: 15, of which 11 were waited for; matrix products, arithmetic and copies ran while one was open for 19% of the time, Pallas kernels for 0%

profile of v2, /device:TPU:0, one launch (start us, length us, event | category | flops | bytes accessed | tf_op | source)
XLA Modules:
  0.0 269.2 jit_solution(18229551373768772815)
XLA Ops:
  13.3 8.7 %convert_reduce_fusion = (f32[16,128]{1,0:T(8,128)S(1)}, bf16[16,8,128,128]{3,1,2,0:T(8,128)(2,1)}) fusion(bf16[128,128,128]{2,1,0:T(8,128)(2,1)} %bitcast.111, s32[16,8]{1,0:T(8,128)S(1)} %multiply_add_fusion, s32[128]{0:T(128)S(1)} %add_bitcast_fusion, pred[128]{0:T(512)(128)(4,1)S(1)} %iota_compare_fusion.3), kind=kOutput, calls=%fused_computation.1 | convolution fusion | flops 541095936 | bytes 8397952 | tf_op jit(solution)/shard_map/sp,sab->pab/dot_general | solution.py:61
  22.1 7.3 %dot_general.50 = bf16[8,256,1024]{2,1,0:T(8,128)(2,1)} reshape(bf16[16,128,8,128]{3,2,1,0:T(8,128)(2,1)} %bitcast.108) | data formatting | bytes 8388608 | tf_op jit(solution)/shard_map/dot_general | solution.py:92
  29.4 2.3 all-gather.6.cloned.1.call-done
  33.0 4.5 %fusion.29 = f32[8,256,512]{2,1,0:T(8,128)S(1)} fusion(bf16[8,256,1024]{2,1,0:T(8,128)(2,1)} %dot_general.50, bf16[1024,512,1]{1,0,2:T(8,128)(2,1)S(1)} %bitcast.115), kind=kOutput, calls=%fused_computation.80 | convolution fusion | flops 2147483648 | bytes 9437184 | tf_op jit(solution)/shard_map/dot_general | solution.py:92
  37.5 2.7 select_maximum_fusion
  42.4 32.6 %all_gather.14 = bf16[256,512]{1,0:T(8,128)(2,1)S(1)} all-gather(bf16[32,512]{1,0:T(8,128)(2,1)S(1)} %slice_bitcast_fusion.2), channel_id=1, replica_groups=mesh['prow'=4,'pcol'=8] {'pcol'}, dimensions={0}, use_global_device_ids=true | all-gather | bytes 294912 | tf_op jit(solution)/shard_map/all_gather | solution.py:76
  75.1 57.8 %reduce-scatter.3.cloned.1.call-done = f32[1,257,512]{2,1,0:T(8,128)} async-done(((f32[8,257,512]{2,1,0:T(8,128)}), f32[1,257,512]{2,1,0:T(8,128)}) %reduce-scatter.3.cloned.1.call-update) | async-done | bytes 526352 | tf_op jit(solution)/shard_map/reduce_scatter | solution.py:100
  138.3 2.9 %collective-permute-done = f32[264192]{0:T(1024)} collective-permute-done((f32[264192]{0:T(1024)}, f32[264192]{0:T(1024)}, u32[]{:S(2)}, u32[]{:S(2)}) %collective-permute-start) | collective-permute-done | bytes 1056800 | tf_op jit(solution)/shard_map/ppermute | solution.py:25
  144.2 12.6 %collective-permute-done.1 = f32[132096]{0:T(1024)S(1)} collective-permute-done((f32[132096]{0:T(1024)S(1)}, f32[132096]{0:T(1024)S(1)}, u32[]{:S(2)}, u32[]{:S(2)}) %collective-permute-start.1) | collective-permute-done | bytes 528416 | tf_op jit(solution)/shard_map/ppermute | solution.py:25
  158.5 6.1 %collective-permute-done.2 = f32[66048]{0:T(1024)S(1)} collective-permute-done((f32[66048]{0:T(1024)S(1)}, f32[66048]{0:T(1024)S(1)}, u32[]{:S(2)}, u32[]{:S(2)}) %collective-permute-start.2) | collective-permute-done | bytes 264224 | tf_op jit(solution)/shard_map/ppermute | solution.py:25
  166.4 3.3 %collective-permute-done.3 = f32[33024]{0:T(1024)S(1)} collective-permute-done((f32[33024]{0:T(1024)S(1)}, f32[33024]{0:T(1024)S(1)}, u32[]{:S(2)}, u32[]{:S(2)}) %collective-permute-start.3) | collective-permute-done | bytes 132128 | tf_op jit(solution)/shard_map/ppermute | solution.py:25
  169.8 2.1 collective-permute-start.4
  171.9 3.4 %collective-permute-done.4 = f32[16512]{0:T(1024)S(1)} collective-permute-done((f32[16512]{0:T(1024)S(1)}, f32[16512]{0:T(1024)S(1)}, u32[]{:S(2)}, u32[]{:S(2)}) %collective-permute-start.4) | collective-permute-done | bytes 66080 | tf_op jit(solution)/shard_map/ppermute | solution.py:25
  175.4 2.2 collective-permute-start.5
  178.7 2.1 collective-permute-done.5
  180.8 2.2 collective-permute-start.6
  183.0 3.0 %collective-permute-done.6 = f32[33024]{0:T(1024)S(1)} collective-permute-done((f32[33024]{0:T(1024)S(1)}, f32[33024]{0:T(1024)S(1)}, u32[]{:S(2)}, u32[]{:S(2)}) %collective-permute-start.6) | collective-permute-done | bytes 132128 | tf_op jit(solution)/shard_map/ppermute | solution.py:29
  188.3 5.1 %all-to-all-start = ((bf16[8,256,4,8]{1,3,2,0:T(8,128)(2,1)}), bf16[8,256,4,8]{1,3,2,0:T(8,128)(2,1)S(1)}, u32[]{:S(2)}, u32[]{:S(2)}) async-start(bf16[8,256,4,8]{1,3,2,0:T(8,128)(2,1)} %copy.33), calls=%async_computation.1 | async-start | bytes 262144 | tf_op jit(solution)/shard_map/all_to_all | solution.py:88
  193.5 5.2 %copy.47 = bf16[256,8,8,128]{3,1,2,0:T(8,128)(2,1)} copy(bf16[256,8,8,128]{3,2,1,0:T(8,128)(2,1)} %bitcast.109) | data formatting | bytes 8388608
  198.7 6.6 %copy.31 = bf16[1024,2048]{1,0:T(8,128)(2,1)} copy(bf16[1024,2048]{0,1:T(8,128)(2,1)} %bitcast.110) | data formatting | bytes 8388608 | tf_op jit(solution)/shard_map/dot_general | solution.py:139
  207.8 21.4 %all-gather.4.cloned.1.call-done = bf16[2048,512]{1,0:T(8,128)(2,1)} async-done(((bf16[256,512]{1,0:T(8,128)(2,1)}), bf16[2048,512]{1,0:T(8,128)(2,1)}) %all-gather.4.cloned.1.call-update) | async-done | bytes 2097168 | tf_op jit(solution)/shard_map/all_gather | solution.py:138
  229.2 5.3 %fusion.5 = bf16[4,256,512]{2,1,0:T(8,128)(2,1)S(1)} fusion(bf16[4,256,2048]{2,1,0:T(8,128)(2,1)} %bitcast.112, bf16[2048,512]{1,0:T(8,128)(2,1)} %all-gather.4.cloned.1.call-done), kind=kOutput, calls=%fused_computation.11 | convolution fusion | flops 2148007936 | bytes 7340032 | tf_op jit(solution)/shard_map/dot_general | solution.py:139
  242.4 2.0 maximum_select_fusion.1
  249.1 10.7 %reduce-scatter.5.cloned.1.call-done = bf16[1,264,512]{2,1,0:T(8,128)(2,1)} async-done(((bf16[4,264,512]{2,1,0:T(8,128)(2,1)}), bf16[1,264,512]{2,1,0:T(8,128)(2,1)}) %reduce-scatter.5.cloned.1.call-update) | async-done | bytes 270352 | tf_op jit(solution)/shard_map/reduce_scatter | solution.py:153
  (99 shorter events, 42.1 us)
Async XLA Ops:
  7.2 127.7 %copy-start = (bf16[512,512]{1,0:T(8,128)(2,1)S(1)}, bf16[512,512]{1,0:T(8,128)(2,1)}, u32[]{:S(2)}) copy-start(bf16[512,512]{1,0:T(8,128)(2,1)} %param.19) | copy-start | bytes 1572868
  7.2 24.5 %all-gather.6.cloned.1.call-start = ((), (), s32[]{:S(2)}) async-start(), calls=%async_computation.6 | async-start | bytes 1351680 | tf_op jit(solution)/shard_map/all_gather | solution.py:73
  11.9 121.0 %reduce-scatter.3.cloned.1.call-start = ((), (), s32[]{:S(2)}) async-start(), calls=%async_computation.3 | async-start | bytes 4866048 | tf_op jit(solution)/shard_map/reduce_scatter | solution.py:100
  40.2 188.9 %all-gather.4.cloned.1.call-start = ((), (), s32[]{:S(2)}) async-start(), calls=%async_computation.4 | async-start | bytes 2359296 | tf_op jit(solution)/shard_map/all_gather | solution.py:138
  41.4 93.5 %copy-start.11 = (bf16[256,512]{1,0:T(8,128)(2,1)S(1)}, bf16[256,512]{1,0:T(8,128)(2,1)}, u32[]{:S(2)}) copy-start(bf16[256,512]{1,0:T(8,128)(2,1)} %param.21) | copy-start | bytes 786436
  41.4 93.5 %copy-start.12 = (f32[512]{0:T(512)S(1)}, f32[512]{0:T(512)}, u32[]{:S(2)}) copy-start(f32[512]{0:T(512)} %param.20) | copy-start | bytes 6148
  138.3 3.0 %collective-permute-start = (f32[264192]{0:T(1024)}, f32[264192]{0:T(1024)}, u32[]{:S(2)}, u32[]{:S(2)}) collective-permute-start(f32[264192]{0:T(1024)} %select_n.212), channel_id=1, source_target_pairs={{0,8},{8,0},{16,24},{24,16},{1,9},{9,1},{17,25},{25,17},{2,10},{10... | collective-permute-start | bytes 3170312 | tf_op jit(solution)/shard_map/ppermute | solution.py:25
  142.7 14.1 %collective-permute-start.1 = (f32[132096]{0:T(1024)S(1)}, f32[132096]{0:T(1024)S(1)}, u32[]{:S(2)}, u32[]{:S(2)}) collective-permute-start(f32[132096]{0:T(1024)S(1)} %slice_select_fusion), channel_id=1, source_target_pairs={{0,16},{8,24},{16,0},{24,8},{1,17},{9,25},{17,1},{25,9},{2,18},{10... | collective-permute-start | bytes 1585160 | tf_op jit(solution)/shard_map/ppermute | solution.py:25
  156.9 7.6 %collective-permute-start.2 = (f32[66048]{0:T(1024)S(1)}, f32[66048]{0:T(1024)S(1)}, u32[]{:S(2)}, u32[]{:S(2)}) collective-permute-start(f32[66048]{0:T(1024)S(1)} %slice_select_fusion.1), channel_id=1, source_target_pairs={{0,1},{1,0},{2,3},{3,2},{4,5},{5,4},{6,7},{7,6},{8,9},{9,8},{10,11... | collective-permute-start | bytes 792584 | tf_op jit(solution)/shard_map/ppermute | solution.py:25
  164.7 5.1 %collective-permute-start.3 = (f32[33024]{0:T(1024)S(1)}, f32[33024]{0:T(1024)S(1)}, u32[]{:S(2)}, u32[]{:S(2)}) collective-permute-start(f32[33024]{0:T(1024)S(1)} %slice_select_fusion.2), channel_id=1, source_target_pairs={{0,2},{1,3},{2,0},{3,1},{4,6},{5,7},{6,4},{7,5},{8,10},{9,11},{10,... | collective-permute-start | bytes 396296 | tf_op jit(solution)/shard_map/ppermute | solution.py:25
  169.8 17.8 %copy-start.9 = (bf16[256,256]{1,0:T(8,128)(2,1)S(1)}, bf16[256,256]{1,0:T(8,128)(2,1)}, u32[]{:S(2)}) copy-start(bf16[256,256]{1,0:T(8,128)(2,1)} %param.17) | copy-start | bytes 393220
  169.8 5.6 %collective-permute-start.4 = (f32[16512]{0:T(1024)S(1)}, f32[16512]{0:T(1024)S(1)}, u32[]{:S(2)}, u32[]{:S(2)}) collective-permute-start(f32[16512]{0:T(1024)S(1)} %slice_select_fusion.3), channel_id=1, source_target_pairs={{0,4},{1,5},{2,6},{3,7},{4,0},{5,1},{6,2},{7,3},{8,12},{9,13},{10,... | collective-permute-start | bytes 198152 | tf_op jit(solution)/shard_map/ppermute | solution.py:25
  175.4 5.4 %collective-permute-start.5 = (f32[16512]{0:T(1024)S(1)}, f32[16512]{0:T(1024)S(1)}, u32[]{:S(2)}, u32[]{:S(2)}) collective-permute-start(f32[16512]{0:T(1024)S(1)} %select_add_fusion.3), channel_id=1, source_target_pairs={{0,4},{1,5},{2,6},{3,7},{4,0},{5,1},{6,2},{7,3},{8,12},{9,13},{10,... | collective-permute-start | bytes 198152 | tf_op jit(solution)/shard_map/ppermute | solution.py:29
  180.8 5.2 %collective-permute-start.6 = (f32[33024]{0:T(1024)S(1)}, f32[33024]{0:T(1024)S(1)}, u32[]{:S(2)}, u32[]{:S(2)}) collective-permute-start(f32[33024]{0:T(1024)S(1)} %maximum_select_fusion.6), channel_id=1, source_target_pairs={{0,2},{1,3},{2,0},{3,1},{4,6},{5,7},{6,4},{7,5},{8,10},{9,11},{10,... | collective-permute-start | bytes 396296 | tf_op jit(solution)/shard_map/ppermute | solution.py:29
  186.0 19.4 %collective-permute-start.7 = (f32[66048]{0:T(1024)S(1)}, f32[66048]{0:T(1024)S(1)}, u32[]{:S(2)}, u32[]{:S(2)}) collective-permute-start(f32[66048]{0:T(1024)S(1)} %maximum_select_fusion.5), channel_id=1, source_target_pairs={{0,1},{1,0},{2,3},{3,2},{4,5},{5,4},{6,7},{7,6},{8,9},{9,8},{10,11... | collective-permute-start | bytes 792584 | tf_op jit(solution)/shard_map/ppermute | solution.py:29
  188.3 17.0 %all-to-all-start = ((bf16[8,256,4,8]{1,3,2,0:T(8,128)(2,1)}), bf16[8,256,4,8]{1,3,2,0:T(8,128)(2,1)S(1)}, u32[]{:S(2)}, u32[]{:S(2)}) async-start(bf16[8,256,4,8]{1,3,2,0:T(8,128)(2,1)} %copy.33), calls=%async_computation.1 | async-start | bytes 262144 | tf_op jit(solution)/shard_map/all_to_all | solution.py:88
  193.5 66.3 %reduce-scatter.5.cloned.1.call-start = ((), (), s32[]{:S(2)}) async-start(), calls=%async_computation.5 | async-start | bytes 1351680 | tf_op jit(solution)/shard_map/reduce_scatter | solution.py:153
  206.2 28.3 %copy-start.3 = (f32[132096]{0:T(1024)}, f32[132096]{0:T(1024)S(1)}, u32[]{:S(2)}) copy-start(f32[132096]{0:T(1024)S(1)} %maximum_select_fusion.4) | copy-start | bytes 1585156
  206.2 29.9 %collective-permute-start.8 = (f32[132096]{0:T(1024)S(1)}, f32[132096]{0:T(1024)S(1)}, u32[]{:S(2)}, u32[]{:S(2)}) collective-permute-start(f32[132096]{0:T(1024)S(1)} %maximum_select_fusion.4), channel_id=1, source_target_pairs={{0,16},{8,24},{16,0},{24,8},{1,17},{9,25},{17,1},{25,9},{2,18},{10... | collective-permute-start | bytes 1585160 | tf_op jit(solution)/shard_map/ppermute | solution.py:29
  229.2 5.3 %copy-start.6 = (bf16[2048,512]{1,0:T(8,128)(2,1)S(1)}, bf16[2048,512]{1,0:T(8,128)(2,1)}, u32[]{:S(2)}) copy-start(bf16[2048,512]{1,0:T(8,128)(2,1)} %all-gather.4.cloned.1.call-done) | copy-start | bytes 6291460
  237.5 6.9 %copy-start.1 = (f32[264192]{0:T(1024)}, f32[264192]{0:T(1024)S(1)}, u32[]{:S(2)}) copy-start(f32[264192]{0:T(1024)S(1)} %maximum_select_fusion.2) | copy-start | bytes 3170308
  237.5 6.9 %collective-permute-start.9 = (f32[264192]{0:T(1024)S(1)}, f32[264192]{0:T(1024)}, u32[]{:S(2)}, u32[]{:S(2)}) collective-permute-start(f32[264192]{0:T(1024)S(1)} %maximum_select_fusion.2), channel_id=1, source_target_pairs={{0,8},{8,0},{16,24},{24,16},{1,9},{9,1},{17,25},{25,17},{2,10},{10... | collective-permute-start | bytes 3170312 | tf_op jit(solution)/shard_map/ppermute | solution.py:29
  247.6 12.2 %copy-start.5 = (bf16[512,512]{1,0:T(8,128)(2,1)S(1)}, bf16[512,512]{1,0:T(8,128)(2,1)}, u32[]{:S(2)}) copy-start(bf16[512,512]{1,0:T(8,128)(2,1)} %param.18) | copy-start | bytes 1572868
  247.6 13.5 %copy-start.10 = (s32[1,1,8]{2,1,0:T(1,128)S(1)}, s32[1,1,8]{2,1,0:T(1,128)}, u32[]{:S(2)}) copy-start(s32[1,1,8]{2,1,0:T(1,128)} %param.16) | copy-start | bytes 100
  (4 other events, 3.8 us)
Sparse Core Ops, SparseCore 0:
  12.1 19.5 all-gather.5
  40.3 92.5 reduce-scatter.2
  178.8 50.2 all-gather.3
  236.2 23.5 reduce-scatter.4
